TPU v7x, 32 devices: a whole 2x2x4 slice. The times are simulated.
32 devices in a mesh: grp: 8 (over y, x, core), sub: 4 (over z).
Axes of the slice: x: 2, y: 2, z: 4, core: 2. Of those that a mesh axis runs over, the one named last changes fastest.
Arguments:
- tokens: bfloat16 [128, 32, 256], P(('grp', 'sub')), may hold values from -64 to 64
- proj_weight: bfloat16 [256, 256], replicated, may hold values from -2 to 2
- match_grad: bfloat16 [4096, 1024], P(('grp', 'sub')), may hold values from -3072 to 3072
- edge_first: int32 [4096], P(('grp', 'sub')), may hold values from 0 to 15, as said below
- pair_second_image: int32 [4096], P(('grp', 'sub')), may hold values from 0 to 31, as said below
- send_pick: int32 [1024], P(('grp', 'sub')), may hold values from 0 to 3, as said below
Outputs:
- token_grad: bfloat16 [128, 32, 256], P(('grp', 'sub'))
Inputs may be any that keep to these rules, and one draw needn't show every extreme that they name: On each device the pairs (edge_first, pair_second_image) are distinct. `pair_second_image`: on each device every receive slot 0 to 31 is named by at least one pair. `send_pick`: for each device and each index p of grp, the 4 entries of its send slots p * 4 to p * 4 + 3 name different images.
All inputs are finite; a program needn't handle non-finite values.
Results may differ from a plain program's by a relative error of at most 0.017.
Values may be sent and summed in bfloat16 or wider, within the bound.
No kernel may reach another device: no remote copies, remote signals or barrier semaphores. Data moves between devices by JAX's collectives and lax.ppermute only.
A program may use at most 64 MiB of HBM per device.

v0:
```python
import jax
import jax.numpy as jnp
from jax import lax
from jax.sharding import PartitionSpec as P

EPSILON = 1e-05
SOFTMAX_COOLING = 0.1


def normalize(token_triple, proj_weight):
    image_count, length, feat_width = token_triple.shape
    feature = jnp.dot(
        token_triple.reshape(image_count * length, feat_width),
        proj_weight,
        preferred_element_type=jnp.float32,
    )
    inv_rms = lax.rsqrt(jnp.mean(feature * feature, axis=-1, keepdims=True) + EPSILON)
    normed = feature * inv_rms
    return (normed, inv_rms, normed.astype(jnp.bfloat16).reshape(image_count, length, feat_width))


def edge_terms(first_image_features, second_feats, match_block):
    score_scale = 1.0 / (first_image_features.shape[-1] * SOFTMAX_COOLING)
    scores = (
        jnp.einsum(
            "eid,ejd->eij", first_image_features, second_feats, preferred_element_type=jnp.float32
        )
        * score_scale
    )
    expo = jnp.exp(scores)
    rows = expo / jnp.sum(expo, axis=2, keepdims=True)
    cols = expo / jnp.sum(expo, axis=1, keepdims=True)
    incoming_gradient = match_block.astype(jnp.float32)
    d_rows = incoming_gradient * cols
    d_cols = incoming_gradient * rows
    d_scores = rows * (d_rows - jnp.sum(d_rows * rows, axis=2, keepdims=True)) + cols * (
        d_cols - jnp.sum(d_cols * cols, axis=1, keepdims=True)
    )
    d_scaled = (d_scores * score_scale).astype(jnp.bfloat16)
    grad_first = jnp.einsum(
        "eij,ejd->eid", d_scaled, second_feats, preferred_element_type=jnp.float32
    )
    grad_second = jnp.einsum(
        "eij,eid->ejd", d_scaled, first_image_features, preferred_element_type=jnp.float32
    )
    return (grad_first, grad_second)


def local(tokens, proj_weight, match_grad, edge_first, pair_second_image, send_pick):
    img_count, length, feat_width = tokens.shape
    normed, inv_rms, normed_b = normalize(tokens, proj_weight)
    raw_pool = lax.all_gather(tokens, "sub", axis=0, tiled=True)
    raw_received = lax.all_to_all(
        jnp.take(tokens, send_pick, axis=0), "grp", split_axis=0, concat_axis=0, tiled=True
    )
    pool = normalize(raw_pool, proj_weight)[2]
    received = normalize(raw_received, proj_weight)[2]
    pool_count = pool.shape[0]
    slot_count = received.shape[0]
    edge_count = edge_first.shape[0]
    grads = match_grad.reshape(edge_count, length, length)
    edge_block = 64

    def block_step(block_index, totals):
        pool_total, slot_total = totals
        block_start = block_index * edge_block
        first_images = lax.dynamic_slice_in_dim(edge_first, block_start, edge_block, 0)
        seconds = lax.dynamic_slice_in_dim(pair_second_image, block_start, edge_block, 0)
        block_grads = lax.dynamic_slice_in_dim(grads, block_start, edge_block, 0)
        grad_first, grad_second = edge_terms(
            jnp.take(pool, first_images, axis=0), jnp.take(received, seconds, axis=0), block_grads
        )
        pool_total = pool_total.at[first_images].add(grad_first)
        slot_total = slot_total.at[seconds].add(grad_second)
        return (pool_total, slot_total)

    start_totals = (
        jnp.zeros((pool_count, length, feat_width), jnp.float32),
        jnp.zeros((slot_count, length, feat_width), jnp.float32),
    )
    pool_total, slot_total = lax.fori_loop(0, edge_count // edge_block, block_step, start_totals)
    returned = lax.all_to_all(
        slot_total.astype(jnp.bfloat16), "grp", split_axis=0, concat_axis=0, tiled=True
    )
    owned = lax.psum_scatter(
        pool_total.astype(jnp.bfloat16), "sub", scatter_dimension=0, tiled=True
    ).astype(jnp.float32)
    pick_onehot = (jnp.arange(img_count, dtype=jnp.int32)[:, None] == send_pick[None, :]).astype(
        jnp.bfloat16
    )
    incoming_gradient = owned + jnp.einsum(
        "ir,rld->ild", pick_onehot, returned, preferred_element_type=jnp.float32
    )
    incoming_gradient = incoming_gradient.reshape(img_count * length, feat_width)
    feature_grad = (
        inv_rms
        * (
            incoming_gradient
            - normed * jnp.mean(incoming_gradient * normed, axis=-1, keepdims=True)
        )
    ).astype(jnp.bfloat16)
    token_grad = jnp.einsum(
        "nk,dk->nd", feature_grad, proj_weight, preferred_element_type=jnp.float32
    )
    return token_grad.astype(jnp.bfloat16).reshape(img_count, length, feat_width)


def solution(mesh):
    placed = (
        P(("grp", "sub"), None, None),
        P(),
        P(("grp", "sub"), None),
        P(("grp", "sub")),
        P(("grp", "sub")),
        P(("grp", "sub")),
    )
    return jax.shard_map(
        local, mesh=mesh, in_specs=placed, out_specs=P(("grp", "sub"), None, None), check_vma=False
    )
```

profile of v0, /device:TPU:0, one launch (start us, length us, event | category | flops | bytes accessed | tf_op | source)
XLA Modules:
  0.0 144.9 jit_solution(10182030258065522187)
XLA Ops:
  6.5 0.7 compare_select_fusion.2
  7.3 0.7 compare_and_fusion.2
  7.9 1.4 gather_fusion.2
  9.4 0.9 broadcast_select_fusion.6
  10.3 5.2 %all-to-all-start = ((bf16[32,32,256]{2,1,0:T(8,128)(2,1)}), bf16[32,32,256]{2,1,0:T(8,128)(2,1)S(1)}, u32[]{:S(2)}, u32[]{:S(2)}) async-start(bf16[32,32,256]{2,1,0:T(8,128)(2,1)} %broadcast_select_fusion.6), calls=%async_computation | async-start | bytes 1048576 | tf_op jit(solution)/shard_map/all_to_all | solution.py:53
  15.5 14.2 %all_gather.3 = bf16[16,32,256]{2,1,0:T(8,128)(2,1)S(1)} all-gather(bf16[4,32,256]{2,1,0:T(8,128)(2,1)S(1)} %copy-done.5), channel_id=1, replica_groups=mesh['grp'=8,'sub'=4] {'sub'}, dimensions={0}, use_global_device_ids=true | all-gather | bytes 327680 | tf_op jit(solution)/shard_map/all_gather | solution.py:52
  29.7 0.9 copy.24
  30.6 0.3 multiply_reduce_fusion.3
  30.9 0.1 multiply_convert_fusion.1
  31.1 0.4 multiply_reduce_fusion.2
  31.5 0.2 multiply_convert_fusion
  31.7 0.1 broadcast_in_dim.81
  31.9 74.0 %while.15 = (s32[]{:T(128)}, f32[16,32,256]{2,1,0:T(8,128)S(1)}, f32[32,32,256]{2,1,0:T(8,128)S(1)}, s32[128]{0:T(128)S(1)}, bf16[16,32,256]{2,1,0:T(8,128)(2,1)...) while((s32[]{:T(128)}, f32[16,32,256]{2,1,0:T(8,128)S(1)}, ...), condition=%wide.region_10.11_spmd, body=%wide.region_3.10_spmd.sunk | while | flops 140456864 | bytes 40517248 | solution.py:81
  32.0 0.7 compare_and_fusion.4
  32.7 1.6 %gather_fusion = bf16[64,32,256]{2,1,0:T(8,128)(2,1)} fusion(bf16[16,32,256]{2,1,0:T(8,128)(2,1)S(1)} %get-tuple-element.284, s32[1024]{0:T(1024)S(1)} %pad_clamp_fusion.5), kind=kCustom, calls=%fused_computation.clone.1 | custom fusion | bytes 2097408 | tf_op jit(solution)/shard_map/while/body/eval_jaxpr/jit(_take)/gather | solution.py:71
  34.3 0.6 gather_fusion.1
  35.0 3.3 %fusion.59 = f32[64,32,32]{2,1,0:T(8,128)} fusion(bf16[64,32,256]{2,1,0:T(8,128)(2,1)} %gather_fusion, pred[64]{0:T(512)(128)(4,1)} %get-tuple-element.253, bf16[64,32,256]{2,1,0:T(8,128)(2,1)S(1)} %gather_fusion.1, pred[64]{0:T(512)(128)(4,1)S(1)} %get-tuple-element.255), kind=kOutput, calls=%fused_computation.9.clone.1 | convolution fusion | flops 34736160 | bytes 2359424 | tf_op jit(solution)/shard_map/while/body/eval_jaxpr/div | solution.py:31
  38.2 2.8 %fusion.58 = f32[64,32,32]{2,1,0:T(8,128)} fusion(bf16[64,32,256]{2,1,0:T(8,128)(2,1)} %gather_fusion, pred[64]{0:T(512)(128)(4,1)S(1)} %copy-done.8, bf16[64,32,256]{2,1,0:T(8,128)(2,1)S(1)} %gather_fusion.1, pred[64]{0:T(512)(128)(4,1)S(1)} %get-tuple-element.255), kind=kOutput, calls=%fused_computation.10.clone.1 | convolution fusion | flops 34736160 | bytes 2359424 | tf_op jit(solution)/shard_map/while/body/eval_jaxpr/div | solution.py:32
  41.1 0.1 constant_dynamic-slice_fusion.2
  41.2 0.8 copy.34
  42.0 2.5 %fusion.60 = f32[64,32,32]{2,1,0:T(8,128)S(1)} fusion(f32[64,32,32]{2,1,0:T(8,128)} %fusion.58, f32[64,32,32]{2,1,0:T(8,128)} %fusion.59, bf16[64,32,32]{2,1,0:T(8,128)(2,1)S(1)} %copy.34), kind=kOutput, calls=%fused_computation.16.clone.1 | output fusion | flops 460831 | bytes 917504 | tf_op jit(solution)/shard_map/while/body/eval_jaxpr/sub | solution.py:37
  44.5 5.0 %fusion.62 = f32[64,32,256]{2,1,0:T(8,128)} fusion(f32[64,32,32]{2,1,0:T(8,128)S(1)} %fusion.60, f32[64,32,32]{2,1,0:T(8,128)} %fusion.59, bf16[64,32,256]{2,1,0:T(8,128)(2,1)} %gather_fusion, pred[64]{0:T(512)(128)(4,1)S(1)} %copy-done.8, f32[64,32,32]{2,1,0:T(8,128)} %fusion.58, bf16[64,32,32]{2,1,0:T(8,128)(2,1)S(1)} %copy.34), kind=kOutput, calls=%fused_computation.28.clone.1 | convolution fusion | flops 34736160 | bytes 4063296 | tf_op jit(solution)/shard_map/while/body/eval_jaxpr/eij,eid->ejd/dot_general | solution.py:43
  49.5 7.0 %scatter_fusion.1 = f32[32,32,256]{2,1,0:T(8,128)S(1)} fusion(f32[32,32,256]{2,1,0:T(8,128)S(1)} %get-tuple-element.270, s32[64]{0:T(128)S(1)} %get-tuple-element.254, f32[64,32,256]{2,1,0:T(8,128)} %fusion.62), kind=kCustom, calls=%fused_computation.4.clone.1 | custom fusion | flops 524288 | bytes 6291712 | tf_op jit(solution)/shard_map/while/body/eval_jaxpr/scatter-add | solution.py:74
  56.6 5.3 %fusion.61 = f32[64,32,256]{2,1,0:T(8,128)} fusion(f32[64,32,32]{2,1,0:T(8,128)S(1)} %fusion.60, f32[64,32,32]{2,1,0:T(8,128)} %fusion.59, bf16[64,32,256]{2,1,0:T(8,128)(2,1)} %copy-done.1, pred[64]{0:T(512)(128)(4,1)S(1)} %get-tuple-element.255, f32[64,32,32]{2,1,0:T(8,128)} %fusion.58, bf16[64,32,32]{2,1,0:T(8,128)(2,1)S(1)} %copy.34), kind=kOutput, calls=%fused_computation.29.clone.1 | convolution fusion | flops 34736160 | bytes 4063296 | tf_op jit(solution)/shard_map/while/body/eval_jaxpr/eij,ejd->eid/dot_general | solution.py:40
  61.9 7.0 %scatter_fusion = f32[16,32,256]{2,1,0:T(8,128)S(1)} fusion(f32[16,32,256]{2,1,0:T(8,128)S(1)} %get-tuple-element.269, s32[64]{0:T(128)S(1)} %get-tuple-element.252, f32[64,32,256]{2,1,0:T(8,128)} %fusion.61), kind=kCustom, calls=%fused_computation.3.clone.1 | custom fusion | flops 524288 | bytes 6291712 | tf_op jit(solution)/shard_map/while/body/eval_jaxpr/scatter-add | solution.py:73
  69.0 0.7 compare_and_fusion.4
  69.7 1.6 %gather_fusion = bf16[64,32,256]{2,1,0:T(8,128)(2,1)} fusion(bf16[16,32,256]{2,1,0:T(8,128)(2,1)S(1)} %get-tuple-element.284, s32[1024]{0:T(1024)S(1)} %pad_clamp_fusion.5), kind=kCustom, calls=%fused_computation.clone.1 | custom fusion | bytes 2097408 | tf_op jit(solution)/shard_map/while/body/eval_jaxpr/jit(_take)/gather | solution.py:71
  71.3 0.6 gather_fusion.1
  71.9 3.3 %fusion.59 = f32[64,32,32]{2,1,0:T(8,128)} fusion(bf16[64,32,256]{2,1,0:T(8,128)(2,1)} %gather_fusion, pred[64]{0:T(512)(128)(4,1)} %get-tuple-element.253, bf16[64,32,256]{2,1,0:T(8,128)(2,1)S(1)} %gather_fusion.1, pred[64]{0:T(512)(128)(4,1)S(1)} %get-tuple-element.255), kind=kOutput, calls=%fused_computation.9.clone.1 | convolution fusion | flops 34736160 | bytes 2359424 | tf_op jit(solution)/shard_map/while/body/eval_jaxpr/div | solution.py:31
  75.2 2.8 %fusion.58 = f32[64,32,32]{2,1,0:T(8,128)} fusion(bf16[64,32,256]{2,1,0:T(8,128)(2,1)} %gather_fusion, pred[64]{0:T(512)(128)(4,1)S(1)} %copy-done.8, bf16[64,32,256]{2,1,0:T(8,128)(2,1)S(1)} %gather_fusion.1, pred[64]{0:T(512)(128)(4,1)S(1)} %get-tuple-element.255), kind=kOutput, calls=%fused_computation.10.clone.1 | convolution fusion | flops 34736160 | bytes 2359424 | tf_op jit(solution)/shard_map/while/body/eval_jaxpr/div | solution.py:32
  78.1 0.1 constant_dynamic-slice_fusion.2
  78.2 0.8 copy.34
  79.0 2.5 %fusion.60 = f32[64,32,32]{2,1,0:T(8,128)S(1)} fusion(f32[64,32,32]{2,1,0:T(8,128)} %fusion.58, f32[64,32,32]{2,1,0:T(8,128)} %fusion.59, bf16[64,32,32]{2,1,0:T(8,128)(2,1)S(1)} %copy.34), kind=kOutput, calls=%fused_computation.16.clone.1 | output fusion | flops 460831 | bytes 917504 | tf_op jit(solution)/shard_map/while/body/eval_jaxpr/sub | solution.py:37
  81.5 5.0 %fusion.62 = f32[64,32,256]{2,1,0:T(8,128)} fusion(f32[64,32,32]{2,1,0:T(8,128)S(1)} %fusion.60, f32[64,32,32]{2,1,0:T(8,128)} %fusion.59, bf16[64,32,256]{2,1,0:T(8,128)(2,1)} %gather_fusion, pred[64]{0:T(512)(128)(4,1)S(1)} %copy-done.8, f32[64,32,32]{2,1,0:T(8,128)} %fusion.58, bf16[64,32,32]{2,1,0:T(8,128)(2,1)S(1)} %copy.34), kind=kOutput, calls=%fused_computation.28.clone.1 | convolution fusion | flops 34736160 | bytes 4063296 | tf_op jit(solution)/shard_map/while/body/eval_jaxpr/eij,eid->ejd/dot_general | solution.py:43
  86.5 7.0 %scatter_fusion.1 = f32[32,32,256]{2,1,0:T(8,128)S(1)} fusion(f32[32,32,256]{2,1,0:T(8,128)S(1)} %get-tuple-element.270, s32[64]{0:T(128)S(1)} %get-tuple-element.254, f32[64,32,256]{2,1,0:T(8,128)} %fusion.62), kind=kCustom, calls=%fused_computation.4.clone.1 | custom fusion | flops 524288 | bytes 6291712 | tf_op jit(solution)/shard_map/while/body/eval_jaxpr/scatter-add | solution.py:74
  93.6 5.3 %fusion.61 = f32[64,32,256]{2,1,0:T(8,128)} fusion(f32[64,32,32]{2,1,0:T(8,128)S(1)} %fusion.60, f32[64,32,32]{2,1,0:T(8,128)} %fusion.59, bf16[64,32,256]{2,1,0:T(8,128)(2,1)} %copy-done.1, pred[64]{0:T(512)(128)(4,1)S(1)} %get-tuple-element.255, f32[64,32,32]{2,1,0:T(8,128)} %fusion.58, bf16[64,32,32]{2,1,0:T(8,128)(2,1)S(1)} %copy.34), kind=kOutput, calls=%fused_computation.29.clone.1 | convolution fusion | flops 34736160 | bytes 4063296 | tf_op jit(solution)/shard_map/while/body/eval_jaxpr/eij,ejd->eid/dot_general | solution.py:40
  98.9 7.0 %scatter_fusion = f32[16,32,256]{2,1,0:T(8,128)S(1)} fusion(f32[16,32,256]{2,1,0:T(8,128)S(1)} %get-tuple-element.269, s32[64]{0:T(128)S(1)} %get-tuple-element.252, f32[64,32,256]{2,1,0:T(8,128)} %fusion.61), kind=kCustom, calls=%fused_computation.3.clone.1 | custom fusion | flops 524288 | bytes 6291712 | tf_op jit(solution)/shard_map/while/body/eval_jaxpr/scatter-add | solution.py:73
  106.0 0.9 convert_element_type.40
  106.8 4.0 %all-to-all-start.1 = ((bf16[32,32,256]{2,1,0:T(8,128)(2,1)}), bf16[32,32,256]{2,1,0:T(8,128)(2,1)S(1)}, u32[]{:S(2)}, u32[]{:S(2)}) async-start(bf16[32,32,256]{2,1,0:T(8,128)(2,1)} %convert_element_type.40), calls=%async_computation.2 | async-start | bytes 1048576 | tf_op jit(solution)/shard_map/all_to_all | solution.py:82
  110.9 0.7 convert_element_type.38
  111.7 0.3 multiply_reduce_fusion.4
  112.0 8.6 %all-to-all-done.1 = bf16[32,32,256]{2,1,0:T(8,128)(2,1)S(1)} async-done(((bf16[32,32,256]{2,1,0:T(8,128)(2,1)}), bf16[32,32,256]{2,1,0:T(8,128)(2,1)S(1)}, u32[]{:S(2)}, u32[]{:S(2)}) %all-to-all-start.1) | async-done | bytes 524320 | tf_op jit(solution)/shard_map/all_to_all | solution.py:82
  120.6 0.4 fusion.31
  121.0 15.0 %reduce-scatter.2.cloned.1.call-done = bf16[4,32,256]{2,1,0:T(8,128)(2,1)} async-done(((bf16[16,32,256]{2,1,0:T(8,128)(2,1)}), bf16[4,32,256]{2,1,0:T(8,128)(2,1)}) %reduce-scatter.2.cloned.1.call-update) | async-done | bytes 65552 | tf_op jit(solution)/shard_map/reduce_scatter | solution.py:85
  136.0 0.9 copy_add_fusion
  136.9 0.2 fusion.33
  137.1 0.1 fusion.35
  137.2 0.8 convolution_convert_fusion
  (55 shorter events, 0.2 us)
Async XLA Ops:
  6.5 24.0 %copy-start = (bf16[256,256]{1,0:T(8,128)(2,1)S(1)}, bf16[256,256]{1,0:T(8,128)(2,1)}, u32[]{:S(2)}) copy-start(bf16[256,256]{1,0:T(8,128)(2,1)} %param.9) | copy-start | bytes 393220
  6.5 8.9 %copy-start.5 = (bf16[4,32,256]{2,1,0:T(8,128)(2,1)S(1)}, bf16[4,32,256]{2,1,0:T(8,128)(2,1)}, u32[]{:S(2)}) copy-start(bf16[4,32,256]{2,1,0:T(8,128)(2,1)} %param.8) | copy-start | bytes 196612
  6.5 23.2 %copy-start.7 = (bf16[128,1024]{1,0:T(8,128)(2,1)S(1)}, bf16[128,1024]{1,0:T(8,128)(2,1)}, u32[]{:S(2)}) copy-start(bf16[128,1024]{1,0:T(8,128)(2,1)} %param.10) | copy-start | bytes 786436
  10.3 20.8 %all-to-all-start = ((bf16[32,32,256]{2,1,0:T(8,128)(2,1)}), bf16[32,32,256]{2,1,0:T(8,128)(2,1)S(1)}, u32[]{:S(2)}, u32[]{:S(2)}) async-start(bf16[32,32,256]{2,1,0:T(8,128)(2,1)} %broadcast_select_fusion.6), calls=%async_computation | async-start | bytes 1048576 | tf_op jit(solution)/shard_map/all_to_all | solution.py:53
  31.1 0.8 copy-start.9
  31.1 0.8 copy-start.11
  32.0 3.0 %copy-start.2 = (bf16[32,32,256]{2,1,0:T(8,128)(2,1)}, bf16[32,32,256]{2,1,0:T(8,128)(2,1)S(1)}, u32[]{:S(2)}) copy-start(bf16[32,32,256]{2,1,0:T(8,128)(2,1)S(1)} %get-tuple-element.286) | copy-start | bytes 1572868 | tf_op jit(solution)/shard_map/while
  34.9 3.3 %copy-start.1 = (bf16[64,32,256]{2,1,0:T(8,128)(2,1)}, bf16[64,32,256]{2,1,0:T(8,128)(2,1)S(1)}, u32[]{:S(2)}) copy-start(bf16[64,32,256]{2,1,0:T(8,128)(2,1)S(1)} %gather_fusion.1) | copy-start | bytes 3145732 | tf_op jit(solution)/shard_map/while
  35.0 3.3 %copy-start.8 = (pred[64]{0:T(512)(128)(4,1)S(1)}, pred[64]{0:T(512)(128)(4,1)}, u32[]{:S(2)}) copy-start(pred[64]{0:T(512)(128)(4,1)} %get-tuple-element.253) | copy-start | bytes 196 | tf_op jit(solution)/shard_map/while
  38.2 2.9 %copy-start.4 = (bf16[128,32,32]{0,2,1:T(8,128)(2,1)S(1)}, bf16[128,32,32]{0,2,1:T(8,128)(2,1)}, u32[]{:S(2)}) copy-start(bf16[128,32,32]{0,2,1:T(8,128)(2,1)} %get-tuple-element.287) | copy-start | bytes 786436 | tf_op jit(solution)/shard_map/while
  61.9 7.0 %copy-start.3 = (bf16[32,32,256]{2,1,0:T(8,128)(2,1)S(1)}, bf16[32,32,256]{2,1,0:T(8,128)(2,1)}, u32[]{:S(2)}) copy-start(bf16[32,32,256]{2,1,0:T(8,128)(2,1)} %copy-done.2) | copy-start | bytes 1572868 | tf_op jit(solution)/shard_map/while
  61.9 7.0 %copy-start.10 = (s32[128]{0:T(128)S(1)}, s32[128]{0:T(128)}, u32[]{:S(2)}) copy-start(s32[128]{0:T(128)} %get-tuple-element.310) | copy-start | bytes 1540 | tf_op jit(solution)/shard_map/while
  61.9 7.1 %copy-start.12 = (s32[128]{0:T(128)S(1)}, s32[128]{0:T(128)}, u32[]{:S(2)}) copy-start(s32[128]{0:T(128)} %get-tuple-element.324) | copy-start | bytes 1540 | tf_op jit(solution)/shard_map/while
  68.9 3.0 %copy-start.2 = (bf16[32,32,256]{2,1,0:T(8,128)(2,1)}, bf16[32,32,256]{2,1,0:T(8,128)(2,1)S(1)}, u32[]{:S(2)}) copy-start(bf16[32,32,256]{2,1,0:T(8,128)(2,1)S(1)} %get-tuple-element.286) | copy-start | bytes 1572868 | tf_op jit(solution)/shard_map/while
  71.9 3.3 %copy-start.1 = (bf16[64,32,256]{2,1,0:T(8,128)(2,1)}, bf16[64,32,256]{2,1,0:T(8,128)(2,1)S(1)}, u32[]{:S(2)}) copy-start(bf16[64,32,256]{2,1,0:T(8,128)(2,1)S(1)} %gather_fusion.1) | copy-start | bytes 3145732 | tf_op jit(solution)/shard_map/while
  71.9 3.3 %copy-start.8 = (pred[64]{0:T(512)(128)(4,1)S(1)}, pred[64]{0:T(512)(128)(4,1)}, u32[]{:S(2)}) copy-start(pred[64]{0:T(512)(128)(4,1)} %get-tuple-element.253) | copy-start | bytes 196 | tf_op jit(solution)/shard_map/while
  75.2 2.9 %copy-start.4 = (bf16[128,32,32]{0,2,1:T(8,128)(2,1)S(1)}, bf16[128,32,32]{0,2,1:T(8,128)(2,1)}, u32[]{:S(2)}) copy-start(bf16[128,32,32]{0,2,1:T(8,128)(2,1)} %get-tuple-element.287) | copy-start | bytes 786436 | tf_op jit(solution)/shard_map/while
  98.9 7.0 %copy-start.3 = (bf16[32,32,256]{2,1,0:T(8,128)(2,1)S(1)}, bf16[32,32,256]{2,1,0:T(8,128)(2,1)}, u32[]{:S(2)}) copy-start(bf16[32,32,256]{2,1,0:T(8,128)(2,1)} %copy-done.2) | copy-start | bytes 1572868 | tf_op jit(solution)/shard_map/while
  98.9 7.1 %copy-start.10 = (s32[128]{0:T(128)S(1)}, s32[128]{0:T(128)}, u32[]{:S(2)}) copy-start(s32[128]{0:T(128)} %get-tuple-element.310) | copy-start | bytes 1540 | tf_op jit(solution)/shard_map/while
  98.9 7.1 %copy-start.12 = (s32[128]{0:T(128)S(1)}, s32[128]{0:T(128)}, u32[]{:S(2)}) copy-start(s32[128]{0:T(128)} %get-tuple-element.324) | copy-start | bytes 1540 | tf_op jit(solution)/shard_map/while
  105.9 5.7 %copy-start.6 = (bf16[4,32,256]{2,1,0:T(8,128)(2,1)S(1)}, bf16[4,32,256]{2,1,0:T(8,128)(2,1)}, u32[]{:S(2)}) copy-start(bf16[4,32,256]{2,1,0:T(8,128)(2,1)} %param.8) | copy-start | bytes 196612
  106.0 14.6 %copy-start.13 = (s32[32]{0:T(128)S(1)}, s32[32]{0:T(128)}, u32[]{:S(2)}) copy-start(s32[32]{0:T(128)} %param.13) | copy-start | bytes 388
  106.8 13.7 %all-to-all-start.1 = ((bf16[32,32,256]{2,1,0:T(8,128)(2,1)}), bf16[32,32,256]{2,1,0:T(8,128)(2,1)S(1)}, u32[]{:S(2)}, u32[]{:S(2)}) async-start(bf16[32,32,256]{2,1,0:T(8,128)(2,1)} %convert_element_type.40), calls=%async_computation.2 | async-start | bytes 1048576 | tf_op jit(solution)/shard_map/all_to_all | solution.py:82
  110.9 25.2 %reduce-scatter.2.cloned.1.call-start = ((), (), s32[]{:S(2)}) async-start(), calls=%async_computation.3 | async-start | bytes 327680 | tf_op jit(solution)/shard_map/reduce_scatter | solution.py:85
Sparse Core Ops, SparseCore 0:
  113.9 22.0 reduce-scatter.1
where the time goes:
time: 146 us; the launch traced here: 145 us
  other arithmetic  40 us (27%)
  matrix products  35 us (24%)
  waiting for transfers between devices  23.7 us (16%)
  blocking collectives  14.2 us (10%)
  between operations  13.6 us (9%)
  starting transfers between devices  9.27 us (6%)
  local copies, waits for them, and re-layouts  8.82 us (6%)
    reduce_scatter x1, waiting for transfers between devices, local(): lax.psum_scatter(pool_total.astype(jnp.bfloat16), 'sub', scatter_dimensio...  15 us
    all_gather x1, blocking collectives, local(): raw_pool = lax.all_gather(tokens, 'sub', axis=0, tiled=True)  14.2 us
    scatter-add x2, other arithmetic, block_step(): slot_total = slot_total.at[seconds].add(grad_second)  14.1 us
    scatter-add x2, other arithmetic, block_step(): pool_total = pool_total.at[first_images].add(grad_first)  14 us
    dot_general x2, matrix products, edge_terms(): jnp.einsum('eij,ejd->eid', d_scaled, second_feats, preferred_element_type...  10.6 us
    dot_general x2, matrix products, edge_terms(): jnp.einsum('eij,eid->ejd', d_scaled, first_image_features, preferred_elem...  10 us
    all_to_all x1, waiting for transfers between devices, local(): lax.all_to_all(slot_total.astype(jnp.bfloat16), 'grp', split_axis=0, conc...  8.62 us
    div x2, matrix products, edge_terms(): rows = expo / jnp.sum(expo, axis=2, keepdims=True)  6.51 us
  transfers between devices with their start and end apart: 3, of which 2 were waited for; matrix products, arithmetic and copies ran while one was open for 2% of the time, Pallas kernels for 0%

commit v1 on v0

--- a/solution.py
+++ b/solution.py
@@ -5,6 +5,12 @@
 
 EPSILON = 1e-05
 SOFTMAX_COOLING = 0.1
+
+
+def shape_things(local_array, on_dim):
+    left_arr = list(local_array.shape[1:])
+    left_arr[on_dim] *= local_array.shape[0]
+    return jnp.moveaxis(local_array, 0, on_dim).reshape(left_arr)
 
 
 def normalize(token_triple, proj_weight):
@@ -49,7 +55,25 @@
 def local(tokens, proj_weight, match_grad, edge_first, pair_second_image, send_pick):
     img_count, length, feat_width = tokens.shape
     normed, inv_rms, normed_b = normalize(tokens, proj_weight)
-    raw_pool = lax.all_gather(tokens, "sub", axis=0, tiled=True)
+    n_peers_all = lax.axis_size("sub")
+    column = tuple(((kk, (kk + 1) % n_peers_all) for kk in range(n_peers_all)))
+    views = tuple(((c, at) for at, c in column))
+    far_arr, u_next = ([], [])
+    pp = 0
+    while pp < n_peers_all - 1:
+        if pp % 2 == 0:
+            y_new = lax.ppermute(far_arr[-1] if far_arr else tokens, "sub", column)
+            far_arr.append(y_new)
+        else:
+            top = lax.ppermute(u_next[-1] if u_next else tokens, axis_name="sub", perm=views)
+            u_next.append(top)
+        pp += 1
+    out_arr = jnp.stack([*far_arr[::-1], tokens, *u_next], axis=0)
+    mid_arr = lax.axis_index("sub")
+    side_arr = len(far_arr)
+    w_next = mid_arr - side_arr
+    out_arr = out_arr[(jnp.arange(n_peers_all) - w_next) % n_peers_all]
+    raw_pool = shape_things(out_arr, 0)
     raw_received = lax.all_to_all(
         jnp.take(tokens, send_pick, axis=0), "grp", split_axis=0, concat_axis=0, tiled=True
     )

time: 146 us -> 141 us (0.966)
  blocking collectives: 14.2 us -> 0 us
  waiting for transfers between devices: 23.7 us -> 29.1 us
  starting transfers between devices: 9.27 us -> 12.6 us
    all_gather x1 -> x0, blocking collectives: 14.2 us -> none  [local(): raw_pool = lax.all_gather(tokens, 'sub', axis=0, tiled=True)]
    ppermute x0 -> x3, waiting for transfers between devices: none -> 6.26 us  [the longest x2 6.26 us: local(): y_new = lax.ppermute(far_arr[-1] if far_arr else tokens, 'sub', column)]
    ppermute x0 -> x3, starting transfers between devices: none -> 5.19 us  [the longest x2 3.11 us: local(): y_new = lax.ppermute(far_arr[-1] if far_arr else tokens, 'sub', column)]
    reduce_scatter x1, waiting for transfers between devices: 15 us -> 12.9 us  [local(): lax.psum_scatter(pool_total.astype(jnp.bfloat16), 'sub', scatter_dimensio...]
  transfers between devices with their start and end apart: 3 -> 6, of which waited for: 2 -> 4; matrix products, arithmetic and copies ran while one was open for 2% -> 5% of each run, Pallas kernels for 0% -> 0%
where the time goes in v1:
time: 141 us; the launch traced here: 140 us
  other arithmetic  40 us (28%)
  matrix products  35 us (25%)
  waiting for transfers between devices  29.1 us (21%)
  between operations  13.6 us (10%)
  starting transfers between devices  12.6 us (9%)
  local copies, waits for them, and re-layouts  9.38 us (7%)
    scatter-add x2, other arithmetic, block_step(): slot_total = slot_total.at[seconds].add(grad_second)  14.1 us
    scatter-add x2, other arithmetic, block_step(): pool_total = pool_total.at[first_images].add(grad_first)  14 us
    reduce_scatter x1, waiting for transfers between devices, local(): lax.psum_scatter(pool_total.astype(jnp.bfloat16), 'sub', scatter_dimensio...  12.9 us
    dot_general x2, matrix products, edge_terms(): jnp.einsum('eij,ejd->eid', d_scaled, second_feats, preferred_element_type...  10.6 us
    dot_general x2, matrix products, edge_terms(): jnp.einsum('eij,eid->ejd', d_scaled, first_image_features, preferred_elem...  10 us
    all_to_all x1, waiting for transfers between devices, local(): lax.all_to_all(slot_total.astype(jnp.bfloat16), 'grp', split_axis=0, conc...  8.55 us
    div x2, matrix products, edge_terms(): rows = expo / jnp.sum(expo, axis=2, keepdims=True)  6.51 us
    ppermute x2, waiting for transfers between devices, local(): y_new = lax.ppermute(far_arr[-1] if far_arr else tokens, 'sub', column)  6.26 us
  transfers between devices with their start and end apart: 6, of which 4 were waited for; matrix products, arithmetic and copies ran while one was open for 5% of the time, Pallas kernels for 0%

profile of v1, /device:TPU:0, one launch (start us, length us, event | category | flops | bytes accessed | tf_op | source)
XLA Modules:
  0.0 139.9 jit_solution(4873073892565318043)
XLA Ops:
  6.5 3.1 %collective-permute-start = (bf16[4,32,256]{2,1,0:T(8,128)(2,1)}, bf16[4,32,256]{2,1,0:T(8,128)(2,1)S(1)}, u32[]{:S(2)}, u32[]{:S(2)}) collective-permute-start(bf16[4,32,256]{2,1,0:T(8,128)(2,1)} %param.8), channel_id=1, source_target_pairs={{0,1},{1,2},{2,3},{3,0},{4,5},{5,6},{6,7},{7,4},{8,9},{9,10},{10,1... | collective-permute-start | bytes 196616 | tf_op jit(solution)/shard_map/ppermute | solution.py:65
  9.6 2.1 %collective-permute-start.2 = (bf16[4,32,256]{2,1,0:T(8,128)(2,1)}, bf16[4,32,256]{2,1,0:T(8,128)(2,1)S(1)}, u32[]{:S(2)}, u32[]{:S(2)}) collective-permute-start(bf16[4,32,256]{2,1,0:T(8,128)(2,1)} %param.8), channel_id=1, source_target_pairs={{1,0},{2,1},{3,2},{0,3},{5,4},{6,5},{7,6},{4,7},{9,8},{10,9},{11,1... | collective-permute-start | bytes 196616 | tf_op jit(solution)/shard_map/ppermute | solution.py:68
  11.7 0.7 compare_select_fusion.2
  12.3 0.7 compare_and_fusion.2
  13.0 1.4 %gather_fusion.3 = bf16[32,32,256]{2,1,0:T(8,128)(2,1)S(1)} fusion(bf16[4,32,256]{2,1,0:T(8,128)(2,1)} %param.8, s32[1024]{0:T(1024)S(1)} %pad_clamp_fusion.2), kind=kCustom, calls=%fused_computation.3 | custom fusion | bytes 1048704 | tf_op jit(solution)/shard_map/jit(_take)/gather | solution.py:78
  14.4 0.9 broadcast_select_fusion.6
  15.3 3.9 %all-to-all-start = ((bf16[32,32,256]{2,1,0:T(8,128)(2,1)}), bf16[32,32,256]{2,1,0:T(8,128)(2,1)S(1)}, u32[]{:S(2)}, u32[]{:S(2)}) async-start(bf16[32,32,256]{2,1,0:T(8,128)(2,1)} %broadcast_select_fusion.6), calls=%async_computation | async-start | bytes 1048576 | tf_op jit(solution)/shard_map/all_to_all | solution.py:77
  19.2 0.9 copy.24
  20.2 6.3 %collective-permute-done.1 = bf16[4,32,256]{2,1,0:T(8,128)(2,1)S(1)} collective-permute-done((bf16[4,32,256]{2,1,0:T(8,128)(2,1)S(1)}, bf16[4,32,256]{2,1,0:T(8,128)(2,1)S(1)}, u32[]{:S(2)}, u32[]{:S(2)}) %collective-permute-start.1) | collective-permute-done | bytes 65568 | tf_op jit(solution)/shard_map/ppermute | solution.py:65
  26.5 0.6 gather_fusion.2
  27.1 0.3 multiply_reduce_fusion.3
  27.4 0.1 multiply_convert_fusion.1
  27.6 1.3 all-to-all-done
  28.9 0.4 multiply_reduce_fusion.2
  29.4 0.2 multiply_convert_fusion
  29.8 74.0 %while.15 = (s32[]{:T(128)}, f32[16,32,256]{2,1,0:T(8,128)S(1)}, f32[32,32,256]{2,1,0:T(8,128)S(1)}, s32[128]{0:T(128)S(1)}, bf16[16,32,256]{2,1,0:T(8,128)(2,1)...) while((s32[]{:T(128)}, f32[16,32,256]{2,1,0:T(8,128)S(1)}, ...), condition=%wide.region_10.11_spmd, body=%wide.region_3.10_spmd.sunk | while | flops 140456864 | bytes 40517248 | solution.py:105
  29.8 0.7 compare_and_fusion.4
  30.5 1.6 %gather_fusion = bf16[64,32,256]{2,1,0:T(8,128)(2,1)} fusion(bf16[16,32,256]{2,1,0:T(8,128)(2,1)S(1)} %get-tuple-element.284, s32[1024]{0:T(1024)S(1)} %pad_clamp_fusion.6), kind=kCustom, calls=%fused_computation.clone.1 | custom fusion | bytes 2097408 | tf_op jit(solution)/shard_map/while/body/eval_jaxpr/jit(_take)/gather | solution.py:95
  32.1 0.6 gather_fusion.1
  32.8 3.3 %fusion.61 = f32[64,32,32]{2,1,0:T(8,128)} fusion(bf16[64,32,256]{2,1,0:T(8,128)(2,1)} %gather_fusion, pred[64]{0:T(512)(128)(4,1)} %get-tuple-element.253, bf16[64,32,256]{2,1,0:T(8,128)(2,1)S(1)} %gather_fusion.1, pred[64]{0:T(512)(128)(4,1)S(1)} %get-tuple-element.255), kind=kOutput, calls=%fused_computation.10.clone.1 | convolution fusion | flops 34736160 | bytes 2359424 | tf_op jit(solution)/shard_map/while/body/eval_jaxpr/div | solution.py:37
  36.1 2.8 %fusion.60 = f32[64,32,32]{2,1,0:T(8,128)} fusion(bf16[64,32,256]{2,1,0:T(8,128)(2,1)} %gather_fusion, pred[64]{0:T(512)(128)(4,1)S(1)} %copy-done.8, bf16[64,32,256]{2,1,0:T(8,128)(2,1)S(1)} %gather_fusion.1, pred[64]{0:T(512)(128)(4,1)S(1)} %get-tuple-element.255), kind=kOutput, calls=%fused_computation.11.clone.1 | convolution fusion | flops 34736160 | bytes 2359424 | tf_op jit(solution)/shard_map/while/body/eval_jaxpr/div | solution.py:38
  39.0 0.8 copy.34
  39.8 2.5 %fusion.62 = f32[64,32,32]{2,1,0:T(8,128)S(1)} fusion(f32[64,32,32]{2,1,0:T(8,128)} %fusion.60, f32[64,32,32]{2,1,0:T(8,128)} %fusion.61, bf16[64,32,32]{2,1,0:T(8,128)(2,1)S(1)} %copy.34), kind=kOutput, calls=%fused_computation.17.clone.1 | output fusion | flops 460831 | bytes 917504 | tf_op jit(solution)/shard_map/while/body/eval_jaxpr/sub | solution.py:43
  42.3 5.0 %fusion.64 = f32[64,32,256]{2,1,0:T(8,128)} fusion(f32[64,32,32]{2,1,0:T(8,128)S(1)} %fusion.62, f32[64,32,32]{2,1,0:T(8,128)} %fusion.61, bf16[64,32,256]{2,1,0:T(8,128)(2,1)} %gather_fusion, pred[64]{0:T(512)(128)(4,1)S(1)} %copy-done.8, f32[64,32,32]{2,1,0:T(8,128)} %fusion.60, bf16[64,32,32]{2,1,0:T(8,128)(2,1)S(1)} %copy.34), kind=kOutput, calls=%fused_computation.29.clone.1 | convolution fusion | flops 34736160 | bytes 4063296 | tf_op jit(solution)/shard_map/while/body/eval_jaxpr/eij,eid->ejd/dot_general | solution.py:49
  47.4 7.0 %scatter_fusion.1 = f32[32,32,256]{2,1,0:T(8,128)S(1)} fusion(f32[32,32,256]{2,1,0:T(8,128)S(1)} %get-tuple-element.270, s32[64]{0:T(128)S(1)} %get-tuple-element.254, f32[64,32,256]{2,1,0:T(8,128)} %fusion.64), kind=kCustom, calls=%fused_computation.5.clone.1 | custom fusion | flops 524288 | bytes 6291712 | tf_op jit(solution)/shard_map/while/body/eval_jaxpr/scatter-add | solution.py:98
  54.4 5.3 %fusion.63 = f32[64,32,256]{2,1,0:T(8,128)} fusion(f32[64,32,32]{2,1,0:T(8,128)S(1)} %fusion.62, f32[64,32,32]{2,1,0:T(8,128)} %fusion.61, bf16[64,32,256]{2,1,0:T(8,128)(2,1)} %copy-done.1, pred[64]{0:T(512)(128)(4,1)S(1)} %get-tuple-element.255, f32[64,32,32]{2,1,0:T(8,128)} %fusion.60, bf16[64,32,32]{2,1,0:T(8,128)(2,1)S(1)} %copy.34), kind=kOutput, calls=%fused_computation.30.clone.1 | convolution fusion | flops 34736160 | bytes 4063296 | tf_op jit(solution)/shard_map/while/body/eval_jaxpr/eij,ejd->eid/dot_general | solution.py:46
  59.7 7.0 %scatter_fusion = f32[16,32,256]{2,1,0:T(8,128)S(1)} fusion(f32[16,32,256]{2,1,0:T(8,128)S(1)} %get-tuple-element.269, s32[64]{0:T(128)S(1)} %get-tuple-element.252, f32[64,32,256]{2,1,0:T(8,128)} %fusion.63), kind=kCustom, calls=%fused_computation.4.clone.1 | custom fusion | flops 524288 | bytes 6291712 | tf_op jit(solution)/shard_map/while/body/eval_jaxpr/scatter-add | solution.py:97
  66.8 0.7 compare_and_fusion.4
  67.5 1.6 %gather_fusion = bf16[64,32,256]{2,1,0:T(8,128)(2,1)} fusion(bf16[16,32,256]{2,1,0:T(8,128)(2,1)S(1)} %get-tuple-element.284, s32[1024]{0:T(1024)S(1)} %pad_clamp_fusion.6), kind=kCustom, calls=%fused_computation.clone.1 | custom fusion | bytes 2097408 | tf_op jit(solution)/shard_map/while/body/eval_jaxpr/jit(_take)/gather | solution.py:95
  69.1 0.6 gather_fusion.1
  69.8 3.3 %fusion.61 = f32[64,32,32]{2,1,0:T(8,128)} fusion(bf16[64,32,256]{2,1,0:T(8,128)(2,1)} %gather_fusion, pred[64]{0:T(512)(128)(4,1)} %get-tuple-element.253, bf16[64,32,256]{2,1,0:T(8,128)(2,1)S(1)} %gather_fusion.1, pred[64]{0:T(512)(128)(4,1)S(1)} %get-tuple-element.255), kind=kOutput, calls=%fused_computation.10.clone.1 | convolution fusion | flops 34736160 | bytes 2359424 | tf_op jit(solution)/shard_map/while/body/eval_jaxpr/div | solution.py:37
  73.0 2.8 %fusion.60 = f32[64,32,32]{2,1,0:T(8,128)} fusion(bf16[64,32,256]{2,1,0:T(8,128)(2,1)} %gather_fusion, pred[64]{0:T(512)(128)(4,1)S(1)} %copy-done.8, bf16[64,32,256]{2,1,0:T(8,128)(2,1)S(1)} %gather_fusion.1, pred[64]{0:T(512)(128)(4,1)S(1)} %get-tuple-element.255), kind=kOutput, calls=%fused_computation.11.clone.1 | convolution fusion | flops 34736160 | bytes 2359424 | tf_op jit(solution)/shard_map/while/body/eval_jaxpr/div | solution.py:38
  76.0 0.8 copy.34
  76.8 2.5 %fusion.62 = f32[64,32,32]{2,1,0:T(8,128)S(1)} fusion(f32[64,32,32]{2,1,0:T(8,128)} %fusion.60, f32[64,32,32]{2,1,0:T(8,128)} %fusion.61, bf16[64,32,32]{2,1,0:T(8,128)(2,1)S(1)} %copy.34), kind=kOutput, calls=%fused_computation.17.clone.1 | output fusion | flops 460831 | bytes 917504 | tf_op jit(solution)/shard_map/while/body/eval_jaxpr/sub | solution.py:43
  79.3 5.0 %fusion.64 = f32[64,32,256]{2,1,0:T(8,128)} fusion(f32[64,32,32]{2,1,0:T(8,128)S(1)} %fusion.62, f32[64,32,32]{2,1,0:T(8,128)} %fusion.61, bf16[64,32,256]{2,1,0:T(8,128)(2,1)} %gather_fusion, pred[64]{0:T(512)(128)(4,1)S(1)} %copy-done.8, f32[64,32,32]{2,1,0:T(8,128)} %fusion.60, bf16[64,32,32]{2,1,0:T(8,128)(2,1)S(1)} %copy.34), kind=kOutput, calls=%fused_computation.29.clone.1 | convolution fusion | flops 34736160 | bytes 4063296 | tf_op jit(solution)/shard_map/while/body/eval_jaxpr/eij,eid->ejd/dot_general | solution.py:49
  84.4 7.0 %scatter_fusion.1 = f32[32,32,256]{2,1,0:T(8,128)S(1)} fusion(f32[32,32,256]{2,1,0:T(8,128)S(1)} %get-tuple-element.270, s32[64]{0:T(128)S(1)} %get-tuple-element.254, f32[64,32,256]{2,1,0:T(8,128)} %fusion.64), kind=kCustom, calls=%fused_computation.5.clone.1 | custom fusion | flops 524288 | bytes 6291712 | tf_op jit(solution)/shard_map/while/body/eval_jaxpr/scatter-add | solution.py:98
  91.4 5.3 %fusion.63 = f32[64,32,256]{2,1,0:T(8,128)} fusion(f32[64,32,32]{2,1,0:T(8,128)S(1)} %fusion.62, f32[64,32,32]{2,1,0:T(8,128)} %fusion.61, bf16[64,32,256]{2,1,0:T(8,128)(2,1)} %copy-done.1, pred[64]{0:T(512)(128)(4,1)S(1)} %get-tuple-element.255, f32[64,32,32]{2,1,0:T(8,128)} %fusion.60, bf16[64,32,32]{2,1,0:T(8,128)(2,1)S(1)} %copy.34), kind=kOutput, calls=%fused_computation.30.clone.1 | convolution fusion | flops 34736160 | bytes 4063296 | tf_op jit(solution)/shard_map/while/body/eval_jaxpr/eij,ejd->eid/dot_general | solution.py:46
  96.7 7.0 %scatter_fusion = f32[16,32,256]{2,1,0:T(8,128)S(1)} fusion(f32[16,32,256]{2,1,0:T(8,128)S(1)} %get-tuple-element.269, s32[64]{0:T(128)S(1)} %get-tuple-element.252, f32[64,32,256]{2,1,0:T(8,128)} %fusion.63), kind=kCustom, calls=%fused_computation.4.clone.1 | custom fusion | flops 524288 | bytes 6291712 | tf_op jit(solution)/shard_map/while/body/eval_jaxpr/scatter-add | solution.py:97
  103.8 0.9 convert_element_type.40
  104.7 3.5 %all-to-all-start.1 = ((bf16[32,32,256]{2,1,0:T(8,128)(2,1)}), bf16[32,32,256]{2,1,0:T(8,128)(2,1)S(1)}, u32[]{:S(2)}, u32[]{:S(2)}) async-start(bf16[32,32,256]{2,1,0:T(8,128)(2,1)} %convert_element_type.40), calls=%async_computation.2 | async-start | bytes 1048576 | tf_op jit(solution)/shard_map/all_to_all | solution.py:106
  108.2 0.7 convert_element_type.38
  109.0 0.3 multiply_reduce_fusion.4
  109.3 8.6 %all-to-all-done.1 = bf16[32,32,256]{2,1,0:T(8,128)(2,1)S(1)} async-done(((bf16[32,32,256]{2,1,0:T(8,128)(2,1)}), bf16[32,32,256]{2,1,0:T(8,128)(2,1)S(1)}, u32[]{:S(2)}, u32[]{:S(2)}) %all-to-all-start.1) | async-done | bytes 524320 | tf_op jit(solution)/shard_map/all_to_all | solution.py:106
  117.8 0.4 fusion.31
  118.2 12.9 %reduce-scatter.2.cloned.1.call-done = bf16[4,32,256]{2,1,0:T(8,128)(2,1)} async-done(((bf16[16,32,256]{2,1,0:T(8,128)(2,1)}), bf16[4,32,256]{2,1,0:T(8,128)(2,1)}) %reduce-scatter.2.cloned.1.call-update) | async-done | bytes 65552 | tf_op jit(solution)/shard_map/reduce_scatter | solution.py:109
  131.1 0.9 copy_add_fusion
  132.0 0.2 fusion.33
  132.3 0.8 convolution_convert_fusion
  (64 shorter events, 0.9 us)
Async XLA Ops:
  6.5 20.5 %copy-start = (bf16[256,256]{1,0:T(8,128)(2,1)S(1)}, bf16[256,256]{1,0:T(8,128)(2,1)}, u32[]{:S(2)}) copy-start(bf16[256,256]{1,0:T(8,128)(2,1)} %param.9) | copy-start | bytes 393220
  6.5 19.9 %copy-start.5 = (bf16[4,32,256]{2,1,0:T(8,128)(2,1)S(1)}, bf16[4,32,256]{2,1,0:T(8,128)(2,1)}, u32[]{:S(2)}) copy-start(bf16[4,32,256]{2,1,0:T(8,128)(2,1)} %param.8) | copy-start | bytes 196612
  6.5 12.7 %copy-start.7 = (bf16[128,1024]{1,0:T(8,128)(2,1)S(1)}, bf16[128,1024]{1,0:T(8,128)(2,1)}, u32[]{:S(2)}) copy-start(bf16[128,1024]{1,0:T(8,128)(2,1)} %param.10) | copy-start | bytes 786436
  6.5 13.6 %collective-permute-start = (bf16[4,32,256]{2,1,0:T(8,128)(2,1)}, bf16[4,32,256]{2,1,0:T(8,128)(2,1)S(1)}, u32[]{:S(2)}, u32[]{:S(2)}) collective-permute-start(bf16[4,32,256]{2,1,0:T(8,128)(2,1)} %param.8), channel_id=1, source_target_pairs={{0,1},{1,2},{2,3},{3,0},{4,5},{5,6},{6,7},{7,4},{8,9},{9,10},{10,1... | collective-permute-start | bytes 196616 | tf_op jit(solution)/shard_map/ppermute | solution.py:65
  9.6 10.6 %collective-permute-start.2 = (bf16[4,32,256]{2,1,0:T(8,128)(2,1)}, bf16[4,32,256]{2,1,0:T(8,128)(2,1)S(1)}, u32[]{:S(2)}, u32[]{:S(2)}) collective-permute-start(bf16[4,32,256]{2,1,0:T(8,128)(2,1)} %param.8), channel_id=1, source_target_pairs={{1,0},{2,1},{3,2},{0,3},{5,4},{6,5},{7,6},{4,7},{9,8},{10,9},{11,1... | collective-permute-start | bytes 196616 | tf_op jit(solution)/shard_map/ppermute | solution.py:68
  15.3 13.6 %all-to-all-start = ((bf16[32,32,256]{2,1,0:T(8,128)(2,1)}), bf16[32,32,256]{2,1,0:T(8,128)(2,1)S(1)}, u32[]{:S(2)}, u32[]{:S(2)}) async-start(bf16[32,32,256]{2,1,0:T(8,128)(2,1)} %broadcast_select_fusion.6), calls=%async_computation | async-start | bytes 1048576 | tf_op jit(solution)/shard_map/all_to_all | solution.py:77
  20.1 6.3 %collective-permute-start.1 = (bf16[4,32,256]{2,1,0:T(8,128)(2,1)S(1)}, bf16[4,32,256]{2,1,0:T(8,128)(2,1)S(1)}, u32[]{:S(2)}, u32[]{:S(2)}) collective-permute-start(bf16[4,32,256]{2,1,0:T(8,128)(2,1)S(1)} %collective-permute-done), channel_id=1, source_target_pairs={{0,1},{1,2},{2,3},{3,0},{4,5},{5,6},{6,7},{7,4},{8,9},{9,10},{10,1... | collective-permute-start | bytes 196616 | tf_op jit(solution)/shard_map/ppermute | solution.py:65
  28.9 0.8 copy-start.9
  28.9 0.8 copy-start.11
  29.8 3.0 %copy-start.2 = (bf16[32,32,256]{2,1,0:T(8,128)(2,1)}, bf16[32,32,256]{2,1,0:T(8,128)(2,1)S(1)}, u32[]{:S(2)}) copy-start(bf16[32,32,256]{2,1,0:T(8,128)(2,1)S(1)} %get-tuple-element.286) | copy-start | bytes 1572868 | tf_op jit(solution)/shard_map/while
  32.8 3.3 %copy-start.1 = (bf16[64,32,256]{2,1,0:T(8,128)(2,1)}, bf16[64,32,256]{2,1,0:T(8,128)(2,1)S(1)}, u32[]{:S(2)}) copy-start(bf16[64,32,256]{2,1,0:T(8,128)(2,1)S(1)} %gather_fusion.1) | copy-start | bytes 3145732 | tf_op jit(solution)/shard_map/while
  32.8 3.3 %copy-start.8 = (pred[64]{0:T(512)(128)(4,1)S(1)}, pred[64]{0:T(512)(128)(4,1)}, u32[]{:S(2)}) copy-start(pred[64]{0:T(512)(128)(4,1)} %get-tuple-element.253) | copy-start | bytes 196 | tf_op jit(solution)/shard_map/while
  36.0 2.9 %copy-start.4 = (bf16[128,32,32]{0,2,1:T(8,128)(2,1)S(1)}, bf16[128,32,32]{0,2,1:T(8,128)(2,1)}, u32[]{:S(2)}) copy-start(bf16[128,32,32]{0,2,1:T(8,128)(2,1)} %get-tuple-element.287) | copy-start | bytes 786436 | tf_op jit(solution)/shard_map/while
  59.7 7.0 %copy-start.3 = (bf16[32,32,256]{2,1,0:T(8,128)(2,1)S(1)}, bf16[32,32,256]{2,1,0:T(8,128)(2,1)}, u32[]{:S(2)}) copy-start(bf16[32,32,256]{2,1,0:T(8,128)(2,1)} %copy-done.2) | copy-start | bytes 1572868 | tf_op jit(solution)/shard_map/while
  59.7 7.0 %copy-start.10 = (s32[128]{0:T(128)S(1)}, s32[128]{0:T(128)}, u32[]{:S(2)}) copy-start(s32[128]{0:T(128)} %get-tuple-element.316) | copy-start | bytes 1540 | tf_op jit(solution)/shard_map/while
  59.7 7.1 %copy-start.12 = (s32[128]{0:T(128)S(1)}, s32[128]{0:T(128)}, u32[]{:S(2)}) copy-start(s32[128]{0:T(128)} %get-tuple-element.330) | copy-start | bytes 1540 | tf_op jit(solution)/shard_map/while
  66.8 3.0 %copy-start.2 = (bf16[32,32,256]{2,1,0:T(8,128)(2,1)}, bf16[32,32,256]{2,1,0:T(8,128)(2,1)S(1)}, u32[]{:S(2)}) copy-start(bf16[32,32,256]{2,1,0:T(8,128)(2,1)S(1)} %get-tuple-element.286) | copy-start | bytes 1572868 | tf_op jit(solution)/shard_map/while
  69.8 3.3 %copy-start.1 = (bf16[64,32,256]{2,1,0:T(8,128)(2,1)}, bf16[64,32,256]{2,1,0:T(8,128)(2,1)S(1)}, u32[]{:S(2)}) copy-start(bf16[64,32,256]{2,1,0:T(8,128)(2,1)S(1)} %gather_fusion.1) | copy-start | bytes 3145732 | tf_op jit(solution)/shard_map/while
  69.8 3.3 %copy-start.8 = (pred[64]{0:T(512)(128)(4,1)S(1)}, pred[64]{0:T(512)(128)(4,1)}, u32[]{:S(2)}) copy-start(pred[64]{0:T(512)(128)(4,1)} %get-tuple-element.253) | copy-start | bytes 196 | tf_op jit(solution)/shard_map/while
  73.0 2.9 %copy-start.4 = (bf16[128,32,32]{0,2,1:T(8,128)(2,1)S(1)}, bf16[128,32,32]{0,2,1:T(8,128)(2,1)}, u32[]{:S(2)}) copy-start(bf16[128,32,32]{0,2,1:T(8,128)(2,1)} %get-tuple-element.287) | copy-start | bytes 786436 | tf_op jit(solution)/shard_map/while
  96.7 7.0 %copy-start.3 = (bf16[32,32,256]{2,1,0:T(8,128)(2,1)S(1)}, bf16[32,32,256]{2,1,0:T(8,128)(2,1)}, u32[]{:S(2)}) copy-start(bf16[32,32,256]{2,1,0:T(8,128)(2,1)} %copy-done.2) | copy-start | bytes 1572868 | tf_op jit(solution)/shard_map/while
  96.7 7.1 %copy-start.10 = (s32[128]{0:T(128)S(1)}, s32[128]{0:T(128)}, u32[]{:S(2)}) copy-start(s32[128]{0:T(128)} %get-tuple-element.316) | copy-start | bytes 1540 | tf_op jit(solution)/shard_map/while
  96.7 7.1 %copy-start.12 = (s32[128]{0:T(128)S(1)}, s32[128]{0:T(128)}, u32[]{:S(2)}) copy-start(s32[128]{0:T(128)} %get-tuple-element.330) | copy-start | bytes 1540 | tf_op jit(solution)/shard_map/while
  103.8 5.2 %copy-start.6 = (bf16[4,32,256]{2,1,0:T(8,128)(2,1)S(1)}, bf16[4,32,256]{2,1,0:T(8,128)(2,1)}, u32[]{:S(2)}) copy-start(bf16[4,32,256]{2,1,0:T(8,128)(2,1)} %param.8) | copy-start | bytes 196612
  103.8 14.0 %copy-start.13 = (s32[32]{0:T(128)S(1)}, s32[32]{0:T(128)}, u32[]{:S(2)}) copy-start(s32[32]{0:T(128)} %param.13) | copy-start | bytes 388
  104.7 13.1 %all-to-all-start.1 = ((bf16[32,32,256]{2,1,0:T(8,128)(2,1)}), bf16[32,32,256]{2,1,0:T(8,128)(2,1)S(1)}, u32[]{:S(2)}, u32[]{:S(2)}) async-start(bf16[32,32,256]{2,1,0:T(8,128)(2,1)} %convert_element_type.40), calls=%async_computation.2 | async-start | bytes 1048576 | tf_op jit(solution)/shard_map/all_to_all | solution.py:106
  108.2 22.9 %reduce-scatter.2.cloned.1.call-start = ((), (), s32[]{:S(2)}) async-start(), calls=%async_computation.3 | async-start | bytes 327680 | tf_op jit(solution)/shard_map/reduce_scatter | solution.py:109
Sparse Core Ops, SparseCore 0:
  111.2 19.8 reduce-scatter.1
